TPU v7x, 256 devices: a whole 4x4x8 slice. The times are simulated.
256 devices in a mesh: expert: 8 (over z_lo, core), tensor: 32 (over z_hi, x, y).
Axes of the slice: x: 4, y: 4, z: 8 (z_hi: 2, z_lo: 4; z = z_hi * 4 + z_lo), core: 2. Of those that a mesh axis runs over, the one named last changes fastest.
Arguments:
- tokens: bfloat16 [2048, 6144], P('expert', 'tensor'), may hold values from -6 to 6
- router_weight: bfloat16 [6144, 8], replicated, may hold values from -0.078125 to 0.078125
- expert_ids: int32 [2048, 2], P('expert'), may hold values from 0 to 7, all different within a row
- w_gate: bfloat16 [8, 6144, 8192], P('expert', None, 'tensor'), may hold values from -0.078125 to 0.078125
- w_up: bfloat16 [8, 6144, 8192], P('expert', None, 'tensor'), may hold values from -0.078125 to 0.078125
- w_down: bfloat16 [8, 8192, 6144], P('expert', 'tensor'), may hold values from -0.125 to 0.125
Outputs:
- moe_out: bfloat16 [2048, 6144], P('expert', 'tensor')
Inputs may be any that keep to these rules, and one draw needn't show every extreme that they name: `expert_ids`: each row names 2 different experts, and every expert is named by some row.
All inputs are finite; a program needn't handle non-finite values.
Results may differ from a plain program's by a relative error of at most 0.03.
Values may be sent and summed in bfloat16 or wider, within the bound.
No kernel may reach another device: no remote copies, remote signals or barrier semaphores. Data moves between devices by JAX's collectives and lax.ppermute only.
A program may use at most 64 MiB of HBM per device.

v0:
```python
import jax
import jax.numpy as jnp
from jax import lax
from jax.sharding import PartitionSpec as P


def body(tokens, router_weight, expert_ids, w_gate, w_up, w_down):
    tok_rows, part_width = tokens.shape
    top_count = expert_ids.shape[1]
    n_experts = lax.axis_size("expert")
    capacity = 5 * tok_rows * top_count // (4 * n_experts)
    slots_all = n_experts * capacity
    gate_local = w_gate[0]
    up_local = w_up[0]
    down_local = w_down[0]
    rows_count = n_experts * capacity
    flat_ids = expert_ids.reshape(-1)
    picks = tok_rows * top_count
    expert_hot = (flat_ids[:, None] == jnp.arange(n_experts, dtype=jnp.int32)[None, :]).astype(
        jnp.float32
    )
    lower = (jnp.arange(picks)[:, None] > jnp.arange(picks)[None, :]).astype(jnp.float32)
    before = jnp.dot(lower, expert_hot, precision=lax.Precision.HIGHEST)
    slot_pos = jnp.sum(before * expert_hot, axis=1).astype(jnp.int32)
    kept = slot_pos < capacity
    target = flat_ids * capacity + slot_pos
    placed = (target[:, None] == jnp.arange(slots_all, dtype=jnp.int32)[None, :]) & kept[:, None]
    placed = placed.reshape(tok_rows, top_count, slots_all).astype(jnp.float32)
    dispatch = jnp.sum(placed, axis=1).astype(jnp.bfloat16)
    contract_first = (((0,), (0,)), ((), ()))
    full_rows = lax.all_gather(tokens, "tensor", axis=1, tiled=True)
    logits = jnp.dot(full_rows, router_weight, preferred_element_type=jnp.float32)
    buckets = lax.dot_general(
        dispatch, full_rows, contract_first, preferred_element_type=jnp.float32
    ).astype(jnp.bfloat16)
    arrived = lax.all_to_all(
        buckets.reshape(n_experts, capacity, -1), "expert", split_axis=0, concat_axis=0, tiled=True
    )
    bucket_rows = arrived.reshape(rows_count, -1)
    gate = jnp.dot(bucket_rows, gate_local, preferred_element_type=jnp.float32)
    upper = jnp.dot(bucket_rows, up_local, preferred_element_type=jnp.float32)
    hidden = (jax.nn.silu(gate) * upper).astype(jnp.bfloat16)
    contract_hidden = (((0,), (1,)), ((), ()))
    summed = lax.psum_scatter(
        lax.dot_general(
            down_local, hidden, contract_hidden, preferred_element_type=jnp.float32
        ).astype(jnp.bfloat16),
        "tensor",
        scatter_dimension=0,
        tiled=True,
    )
    returned = lax.all_to_all(summed, "expert", split_axis=1, concat_axis=1, tiled=True)
    choose_hot = (
        expert_ids[:, :, None] == jnp.arange(n_experts, dtype=jnp.int32)[None, None, :]
    ).astype(jnp.float32)
    chosen = jnp.sum(choose_hot * logits[:, None, :], axis=2)
    weight = jax.nn.sigmoid(chosen - jnp.flip(chosen, axis=1)).astype(jnp.bfloat16)
    combine = jnp.sum(placed * weight.astype(jnp.float32)[:, :, None], axis=1).astype(jnp.bfloat16)
    mixed = lax.dot_general(
        combine, returned, (((1,), (1,)), ((), ())), preferred_element_type=jnp.float32
    )
    return mixed.astype(jnp.bfloat16)


def solution(mesh):
    in_specs = (
        P("expert", "tensor"),
        P(),
        P("expert", None),
        P("expert", None, "tensor"),
        P("expert", None, "tensor"),
        P("expert", "tensor", None),
    )
    out_specs = P("expert", "tensor")
    return jax.shard_map(body, mesh=mesh, in_specs=in_specs, out_specs=out_specs, check_vma=False)
```

profile of v0, /device:TPU:1, one launch (start us, length us, event | category | flops | bytes accessed | tf_op | source)
XLA Modules:
  0.0 633.0 jit_solution(9283036379071454045)
XLA Ops:
  6.5 0.0 copy-start
  6.5 0.0 copy-start.2
  6.5 0.0 all-gather.2.cloned.1.call-start
  6.5 0.7 all-gather.2.cloned.1.call-update
  7.3 0.0 reduce-scatter.4.cloned.1.call-start
  7.3 1.0 copy.26
  8.3 0.1 eq.42
  8.4 0.3 fusion.13
  8.7 0.1 convert_element_type.47
  8.9 0.1 copy.27
  8.9 0.7 multiply_add_fusion
  9.6 101.0 %all-gather.2.cloned.1.call-done = bf16[256,6144]{0,1:T(8,128)(2,1)} async-done(((bf16[256,192]{0,1:T(8,128)(2,1)}), bf16[256,6144]{0,1:T(8,128)(2,1)}) %all-gather.2.cloned.1.call-update) | async-done | bytes 3145744 | tf_op jit(solution)/shard_map/all_gather | solution.py:31
  110.6 2.4 fusion.22
  113.0 0.0 copy-done.2
  113.1 0.1 rev.4
  113.2 0.4 select_reduce_fusion
  113.6 4.2 convolution_convert_fusion.1
  117.8 0.0 copy-start.3
  117.8 179.8 %all_to_all.17 = bf16[8,80,6144]{2,1,0:T(8,128)(2,1)S(1)} all-to-all(bf16[8,80,6144]{2,1,0:T(8,128)(2,1)S(1)} %bitcast.30), channel_id=1, replica_groups=mesh['expert'=8,'tensor'=32] {'expert'}, dimensions={0} | all-to-all | bytes 15728640 | tf_op jit(solution)/shard_map/all_to_all | solution.py:36
  297.6 0.0 copy-start.1
  297.6 3.2 copy-done.1
  300.7 0.0 copy-done.3
  300.7 3.0 fusion.4
  303.8 0.0 copy-done
  303.8 16.6 %fusion = bf16[6144,640]{0,1:T(8,128)(2,1)} fusion(bf16[1,256,6144]{2,1,0:T(8,128)(2,1)S(1)} %copy-done, bf16[640,6144]{1,0:T(8,128)(2,1)} %bitcast.32, bf16[1,6144,256]{2,1,0:T(8,128)(2,1)} %param.10, f32[640,256]{1,0:T(8,128)} %fusion.4), kind=kOutput, calls=%fused_computation.2 | convolution fusion | flops 4031447040 | bytes 22675456 | tf_op jit(solution)/shard_map/dot_general | solution.py:45
  320.4 10.6 %copy.29 = bf16[6144,640]{1,0:T(8,128)(2,1)} copy(bf16[6144,640]{0,1:T(8,128)(2,1)} %fusion) | data formatting | bytes 15728640
  331.0 0.0 reduce-scatter.4.cloned.1.call-update
  331.0 274.8 %reduce-scatter.4.cloned.1.call-done = bf16[192,640]{1,0:T(8,128)(2,1)} async-done(((bf16[6144,640]{1,0:T(8,128)(2,1)}), bf16[192,640]{1,0:T(8,128)(2,1)}) %reduce-scatter.4.cloned.1.call-update) | async-done | bytes 245776
  605.8 1.8 copy.30
  607.7 17.5 %all_to_all.18 = bf16[192,8,80]{0,2,1:T(8,128)(2,1)S(1)} all-to-all(bf16[192,8,80]{0,2,1:T(8,128)(2,1)} %bitcast.34), channel_id=1, replica_groups=mesh['expert'=8,'tensor'=32] {'expert'}, dimensions={1} | all-to-all | bytes 491520 | tf_op jit(solution)/shard_map/all_to_all | solution.py:52
  625.2 1.0 convolution_convert_fusion.2
  (4 shorter events, 0.0 us)
Async XLA Ops:
  6.5 297.2 %copy-start = (bf16[1,256,6144]{2,1,0:T(8,128)(2,1)S(1)}, bf16[1,256,6144]{2,1,0:T(8,128)(2,1)}, u32[]{:S(2)}) copy-start(bf16[1,256,6144]{2,1,0:T(8,128)(2,1)} %param.11) | copy-start | bytes 9437188
  6.5 106.5 %copy-start.2 = (s32[256,2]{0,1:T(2,128)S(1)}, s32[256,2]{0,1:T(2,128)}, u32[]{:S(2)}) copy-start(s32[256,2]{0,1:T(2,128)} %param.8) | copy-start | bytes 6148
  6.5 104.1 %all-gather.2.cloned.1.call-start = ((), (), s32[]{:S(2)}) async-start(), calls=%async_computation.3 | async-start | bytes 3244032 | tf_op jit(solution)/shard_map/all_gather | solution.py:31
  7.3 598.6 %reduce-scatter.4.cloned.1.call-start = ((), (), s32[]{:S(2)}) async-start(), calls=%async_computation.4 | async-start | bytes 8110080
  117.8 183.0 %copy-start.3 = (bf16[1,6144,256]{2,1,0:T(8,128)(2,1)S(1)}, bf16[1,6144,256]{2,1,0:T(8,128)(2,1)}, u32[]{:S(2)}) copy-start(bf16[1,6144,256]{2,1,0:T(8,128)(2,1)} %param.9) | copy-start | bytes 9437188
  297.6 3.2 copy-start.1
Sparse Core Ops, SparseCore 0:
  10.7 99.8 all-gather.1
  331.1 274.6 reduce-scatter.3
where the time goes:
time: 633 us
  waiting for transfers between devices  377 us (60%)
  blocking collectives  197 us (31%)
  matrix products  27.4 us (4%)
  local copies, waits for them, and re-layouts  17 us (3%)
  between operations  13.5 us (2%)
    unnamed x3, waiting for transfers between devices  276 us
    all_to_all x1, blocking collectives, body(): lax.all_to_all(buckets.reshape(n_experts, capacity, -1), 'expert', split_...  180 us
    all_gather x1, waiting for transfers between devices, body(): full_rows = lax.all_gather(tokens, 'tensor', axis=1, tiled=True)  101 us
    all_to_all x1, blocking collectives, body(): lax.all_to_all(summed, 'expert', split_axis=1, concat_axis=1, tiled=True)  17.5 us
    dot_general x1, matrix products, body(): lax.dot_general(down_local, hidden, contract_hidden, preferred_element_ty...  16.6 us
    unnamed x11, local copies, waits for them, and re-layouts  16.6 us
  transfers between devices with their start and end apart: 2, of which 2 were waited for; matrix products, arithmetic and copies ran while one was open for 0% of the time, Pallas kernels for 0%

commit v1 on v0

--- a/solution.py
+++ b/solution.py
@@ -28,7 +28,9 @@
     placed = placed.reshape(tok_rows, top_count, slots_all).astype(jnp.float32)
     dispatch = jnp.sum(placed, axis=1).astype(jnp.bfloat16)
     contract_first = (((0,), (0,)), ((), ()))
-    full_rows = lax.all_gather(tokens, "tensor", axis=1, tiled=True)
+    full_rows = jnp.concatenate(
+        lax.all_to_all(jnp.stack([tokens] * lax.axis_size("tensor")), "tensor", 0, 0), axis=1
+    )
     logits = jnp.dot(full_rows, router_weight, preferred_element_type=jnp.float32)
     buckets = lax.dot_general(
         dispatch, full_rows, contract_first, preferred_element_type=jnp.float32

time: 633 us -> 618 us (0.976)
  waiting for transfers between devices: 377 us -> 324 us
  blocking collectives: 197 us -> 218 us
  starting transfers between devices: 0.04 us -> 14.8 us
    all_gather x1 -> x0, waiting for transfers between devices: 101 us -> none  [body(): full_rows = lax.all_gather(tokens, 'tensor', axis=1, tiled=True)]
    all_to_all x0 -> x1, waiting for transfers between devices: none -> 48.8 us  [body(): lax.all_to_all(jnp.stack([tokens] * lax.axis_size('tensor')), 'tensor', 0...]
    all_to_all x1, blocking collectives: 180 us -> 201 us  [body(): lax.all_to_all(buckets.reshape(n_experts, capacity, -1), 'expert', split_...]
    all_to_all x0 -> x1, starting transfers between devices: none -> 14.7 us  [body(): lax.all_to_all(jnp.stack([tokens] * lax.axis_size('tensor')), 'tensor', 0...]
    unnamed x11 -> x13, local copies, waits for them, and re-layouts: 16.6 us -> 15.8 us
    unnamed x3 -> x2, waiting for transfers between devices: 276 us -> 275 us
where the time goes in v1:
time: 618 us; the launch traced here: 617 us
  waiting for transfers between devices  324 us (52%)
  blocking collectives  218 us (35%)
  matrix products  27.4 us (4%)
  local copies, waits for them, and re-layouts  19.3 us (3%)
  starting transfers between devices  14.8 us (2%)
  between operations  13.5 us (2%)
    unnamed x2, waiting for transfers between devices  275 us
    all_to_all x1, blocking collectives, body(): lax.all_to_all(buckets.reshape(n_experts, capacity, -1), 'expert', split_...  201 us
    all_to_all x1, waiting for transfers between devices, body(): lax.all_to_all(jnp.stack([tokens] * lax.axis_size('tensor')), 'tensor', 0...  48.8 us
    all_to_all x1, blocking collectives, body(): lax.all_to_all(summed, 'expert', split_axis=1, concat_axis=1, tiled=True)  17.5 us
    dot_general x1, matrix products, body(): lax.dot_general(down_local, hidden, contract_hidden, preferred_element_ty...  16.6 us
    unnamed x13, local copies, waits for them, and re-layouts  15.8 us
    all_to_all x1, starting transfers between devices, body(): lax.all_to_all(jnp.stack([tokens] * lax.axis_size('tensor')), 'tensor', 0...  14.7 us
  transfers between devices with their start and end apart: 2, of which 2 were waited for; matrix products, arithmetic and copies ran while one was open for 0% of the time, Pallas kernels for 0%

profile of v1, /device:TPU:1, one launch (start us, length us, event | category | flops | bytes accessed | tf_op | source)
XLA Modules:
  0.0 617.4 jit_solution(6173137816769787662)
XLA Ops:
  6.5 0.0 copy-start
  6.5 3.1 stack.2
  9.6 0.0 copy-start.3
  9.6 0.0 copy-start.2
  9.6 14.7 %all-to-all-start = ((bf16[32,256,192]{1,2,0:T(8,128)(2,1)}), bf16[32,256,192]{1,2,0:T(8,128)(2,1)}, u32[]{:S(2)}, u32[]{:S(2)}) async-start(bf16[32,256,192]{1,2,0:T(8,128)(2,1)} %stack.2), calls=%async_computation | async-start | bytes 6291456 | tf_op jit(solution)/shard_map/all_to_all | solution.py:32
  24.4 0.0 reduce-scatter.4.cloned.1.call-start
  24.4 0.0 copy-done.3
  24.4 0.1 copy.27
  24.6 0.1 eq.42
  24.7 0.3 fusion.13
  25.0 0.1 convert_element_type.47
  25.2 0.1 copy.28
  25.2 48.8 %all-to-all-done = bf16[32,256,192]{1,2,0:T(8,128)(2,1)} async-done(((bf16[32,256,192]{1,2,0:T(8,128)(2,1)}), bf16[32,256,192]{1,2,0:T(8,128)(2,1)}, u32[]{:S(2)}, u32[]{:S(2)}) %all-to-all-start) | async-done | bytes 3145760 | tf_op jit(solution)/shard_map/all_to_all | solution.py:32
  74.1 0.0 copy-done.2
  74.1 2.4 fusion.22
  76.5 0.1 rev.4
  76.6 0.4 select_reduce_fusion
  77.0 4.2 convolution_convert_fusion.1
  81.2 0.0 copy-start.4
  81.2 200.7 %all_to_all.22 = bf16[8,80,6144]{2,1,0:T(8,128)(2,1)S(1)} all-to-all(bf16[8,80,6144]{2,1,0:T(8,128)(2,1)S(1)} %bitcast.33), channel_id=1, replica_groups=mesh['expert'=8,'tensor'=32] {'expert'}, dimensions={0} | all-to-all | bytes 15728640 | tf_op jit(solution)/shard_map/all_to_all | solution.py:38
  281.9 0.0 copy-start.1
  281.9 3.2 copy-done.1
  285.1 0.0 copy-done.4
  285.1 3.0 fusion.4
  288.1 0.0 copy-done
  288.1 16.6 %fusion = bf16[6144,640]{0,1:T(8,128)(2,1)} fusion(bf16[1,256,6144]{2,1,0:T(8,128)(2,1)S(1)} %copy-done, bf16[640,6144]{1,0:T(8,128)(2,1)} %bitcast.35, bf16[1,6144,256]{2,1,0:T(8,128)(2,1)} %param.10, f32[640,256]{1,0:T(8,128)} %fusion.4), kind=kOutput, calls=%fused_computation.2 | convolution fusion | flops 4031447040 | bytes 22675456 | tf_op jit(solution)/shard_map/dot_general | solution.py:47
  304.7 10.6 %copy.30 = bf16[6144,640]{1,0:T(8,128)(2,1)} copy(bf16[6144,640]{0,1:T(8,128)(2,1)} %fusion) | data formatting | bytes 15728640
  315.4 0.0 reduce-scatter.4.cloned.1.call-update
  315.4 274.8 %reduce-scatter.4.cloned.1.call-done = bf16[192,640]{1,0:T(8,128)(2,1)} async-done(((bf16[6144,640]{1,0:T(8,128)(2,1)}), bf16[192,640]{1,0:T(8,128)(2,1)}) %reduce-scatter.4.cloned.1.call-update) | async-done | bytes 245776
  590.2 1.8 copy.31
  592.0 17.5 %all_to_all.23 = bf16[192,8,80]{0,2,1:T(8,128)(2,1)S(1)} all-to-all(bf16[192,8,80]{0,2,1:T(8,128)(2,1)} %bitcast.37), channel_id=1, replica_groups=mesh['expert'=8,'tensor'=32] {'expert'}, dimensions={1} | all-to-all | bytes 491520 | tf_op jit(solution)/shard_map/all_to_all | solution.py:54
  609.6 1.0 convolution_convert_fusion.2
  (5 shorter events, 0.0 us)
Async XLA Ops:
  6.5 281.6 %copy-start = (bf16[1,256,6144]{2,1,0:T(8,128)(2,1)S(1)}, bf16[1,256,6144]{2,1,0:T(8,128)(2,1)}, u32[]{:S(2)}) copy-start(bf16[1,256,6144]{2,1,0:T(8,128)(2,1)} %param.11) | copy-start | bytes 9437188
  9.6 14.8 %copy-start.3 = (s32[256,2]{0,1:T(2,128)S(1)}, s32[256,2]{0,1:T(2,128)}, u32[]{:S(2)}) copy-start(s32[256,2]{0,1:T(2,128)} %param.8) | copy-start | bytes 6148
  9.6 64.4 %copy-start.2 = (bf16[6144,8]{0,1:T(8,128)(2,1)S(1)}, bf16[6144,8]{0,1:T(8,128)(2,1)}, u32[]{:S(2)}) copy-start(bf16[6144,8]{0,1:T(8,128)(2,1)} %param.7) | copy-start | bytes 294916
  9.6 64.4 %all-to-all-start = ((bf16[32,256,192]{1,2,0:T(8,128)(2,1)}), bf16[32,256,192]{1,2,0:T(8,128)(2,1)}, u32[]{:S(2)}, u32[]{:S(2)}) async-start(bf16[32,256,192]{1,2,0:T(8,128)(2,1)} %stack.2), calls=%async_computation | async-start | bytes 6291456 | tf_op jit(solution)/shard_map/all_to_all | solution.py:32
  24.4 565.8 %reduce-scatter.4.cloned.1.call-start = ((), (), s32[]{:S(2)}) async-start(), calls=%async_computation.4 | async-start | bytes 8110080
  81.2 203.9 %copy-start.4 = (bf16[1,6144,256]{2,1,0:T(8,128)(2,1)S(1)}, bf16[1,6144,256]{2,1,0:T(8,128)(2,1)}, u32[]{:S(2)}) copy-start(bf16[1,6144,256]{2,1,0:T(8,128)(2,1)} %param.9) | copy-start | bytes 9437188
  281.9 3.2 copy-start.1
Sparse Core Ops, SparseCore 0:
  315.5 274.6 reduce-scatter.3
